TPU v7x, 32 devices: a whole 2x2x4 slice. The times are simulated.
32 devices in a mesh: nets: 8 (over z, x), region: 4 (over y, core).
Axes of the slice: x: 2, y: 2, z: 4, core: 2. Of those that a mesh axis runs over, the one named last changes fastest.
Arguments:
- logits: float32 [8192, 256], P('nets'), may hold values from -24 to 465
- tile_values: bfloat16 [8, 4, 384, 128, 128], P('nets', 'region'), may hold values from 0 to 1
- tile_pattern: int32 [8, 4, 384], P('nets', 'region'), may hold values from 0 to 2047
- tile_edge: int32 [8, 4, 384], P('nets', 'region'), may hold values from 0 to 63
- tile_counts: int32 [8, 4, 8], P('nets', 'region'), may hold values from 12 to 48, as said below
- capacity: int32 [4, 65536], P('region', 'nets'), may hold values from 0 to 2
Outputs:
- logit_grad: float32 [8192, 256], P('nets')
- usage: float32 [4, 65536], P('region', 'nets')
Inputs may be any that keep to these rules, and one draw needn't show every extreme that they name: `tile_counts`: each entry is at most 48; in every draw some owner receives 48 live slots from every group of a region, and every group has a full owner in every region.
All inputs are finite; a program needn't handle non-finite values.
Results may differ from a plain program's by a relative error of at most 0.0011.
Values may be sent and summed in bfloat16 or wider, within the bound.
No kernel may reach another device: no remote copies, remote signals or barrier semaphores. Data moves between devices by JAX's collectives and lax.ppermute only.
A program may use at most 64 MiB of HBM per device.

v0:
```python
import jax
import jax.numpy as jnp
from jax import lax
from jax.sharding import PartitionSpec as P


def shards(logits, tile_values, tile_pattern, tile_edge, tile_counts, capacity):
    groups = lax.axis_size("nets")
    tile_block = tile_values[0, 0]
    tile_count = tile_block.shape[0]
    block_size = tile_block.shape[1]
    slot_count = tile_count // groups
    pattern_idx = tile_pattern[0, 0]
    edge_idx = tile_edge[0, 0]
    counts = tile_counts[0, 0]
    live_slot = (jnp.arange(slot_count, dtype=jnp.int32)[None, :] < counts[:, None]).reshape(
        tile_count
    )
    weight_live = live_slot.astype(jnp.float32)
    probs = jax.nn.softmax(logits, axis=-1)
    probs_half = probs.astype(jnp.bfloat16).reshape(-1, block_size)
    picked = probs_half[pattern_idx]
    contrib = (
        jnp.einsum("tq,tqe->te", picked, tile_block, preferred_element_type=jnp.float32)
        * weight_live[:, None]
    )
    capacity_f = capacity.reshape(-1, block_size).astype(jnp.float32)
    owned_blocks = capacity_f.shape[0]
    owner_idx = jnp.arange(tile_count, dtype=jnp.int32) // slot_count
    target = owner_idx * owned_blocks + edge_idx
    partial_value = (
        jnp.zeros((groups * owned_blocks, block_size), jnp.float32).at[target].add(contrib)
    )
    usage_edges = lax.psum_scatter(partial_value, "nets", scatter_dimension=0, tiled=True)
    edge_grad = jax.nn.sigmoid(usage_edges - capacity_f).astype(jnp.bfloat16)
    all_grads = lax.all_gather(edge_grad, "nets", axis=0, tiled=True)
    slot_grads = all_grads[target]
    dp_tiles = (
        jnp.einsum("tqe,te->tq", tile_block, slot_grads, preferred_element_type=jnp.float32)
        * weight_live[:, None]
    )
    local_grad = (
        jnp.zeros((probs_half.shape[0], block_size), jnp.float32).at[pattern_idx].add(dp_tiles)
    )
    summed_grad = lax.psum(local_grad.reshape(logits.shape), "region")
    logit_grad = probs * (summed_grad - jnp.sum(probs * summed_grad, axis=-1, keepdims=True))
    return (logit_grad, usage_edges.reshape(capacity.shape))


def solution(mesh):
    in_specs = (
        P("nets", None),
        P("nets", "region", None, None, None),
        P("nets", "region", None),
        P("nets", "region", None),
        P("nets", "region", None),
        P("region", "nets"),
    )
    out_specs = (P("nets", None), P("region", "nets"))
    return jax.shard_map(shards, mesh=mesh, in_specs=in_specs, out_specs=out_specs, check_vma=False)
```

profile of v0, /device:TPU:0, one launch (start us, length us, event | category | flops | bytes accessed | tf_op | source)
XLA Modules:
  0.0 181.0 jit_solution(4683535861114849851)
XLA Ops:
  7.2 0.0 reduce-scatter.2.cloned.1.call-start
  7.2 0.7 fusion.17
  7.9 0.7 fusion.18
  8.6 1.4 reduce_max.9
  10.1 1.6 fusion.5
  11.7 0.7 fusion.16
  12.4 0.1 reshape.122
  12.5 1.6 fusion.21
  14.0 0.0 copy-start.1
  14.1 0.2 reshape.119
  14.2 1.4 gather_fusion
  15.7 6.4 %fusion.2 = f32[384,1,128]{2,1,0:T(1,128)S(1)} fusion(bf16[1,1,384,128,128]{4,3,2,1,0:T(8,128)(2,1)} %param.7, bf16[384,128,1]{1,0,2:T(8,128)(2,1)S(1)} %bitcast.18), kind=kOutput, calls=%fused_computation.6 | convolution fusion | flops 12582912 | bytes 12877824 | tf_op jit(solution)/shard_map/tq,tqe->te/dot_general | solution.py:24
  22.1 0.0 copy-start
  22.1 2.6 %scatter_custom_fusion = f32[512,128]{1,0:T(8,128)} fusion(s32[384]{0:T(512)S(1)} %fusion.18, f32[384,128]{1,0:T(8,128)S(1)} %bitcast.19, f32[]{:T(128)} %constant.11.clone.1, f32[384]{0:T(512)S(1)} %reshape.122), kind=kCustom, calls=%fused_computation.18 | custom fusion | flops 98304 | bytes 460804 | tf_op jit(solution)/shard_map/scatter-add | solution.py:32
  24.7 0.0 reduce-scatter.2.cloned.1.call-update
  24.7 0.0 all-reduce.2.cloned.1.call-start
  24.8 0.0 copy-done.1
  24.8 64.0 %reduce-scatter.2.cloned.1.call-done = f32[64,128]{1,0:T(8,128)} async-done(((f32[512,128]{1,0:T(8,128)}), f32[64,128]{1,0:T(8,128)}) %reduce-scatter.2.cloned.1.call-update) | async-done | bytes 32784 | tf_op jit(solution)/shard_map/reduce_scatter | solution.py:34
  88.8 0.8 divide_convert_fusion
  89.6 30.5 %all_gather.3 = bf16[512,128]{1,0:T(8,128)(2,1)S(1)} all-gather(bf16[64,128]{1,0:T(8,128)(2,1)S(1)} %divide_convert_fusion), channel_id=1, replica_groups=mesh['nets'=8,'region'=4] {'nets'}, dimensions={0}, use_global_device_ids=true | all-gather | bytes 147456 | tf_op jit(solution)/shard_map/all_gather | solution.py:36
  120.1 1.4 gather_fusion.1
  121.6 9.5 %fusion = f32[384,1,128]{2,1,0:T(1,128)S(1)} fusion(bf16[1,1,384,128,128]{4,3,2,1,0:T(8,128)(2,1)} %param.7, bf16[384,128,1]{1,0,2:T(8,128)(2,1)S(1)} %bitcast.20), kind=kOutput, calls=%fused_computation.4 | convolution fusion | flops 12582912 | bytes 12877824 | tf_op jit(solution)/shard_map/tqe,te->tq/dot_general | solution.py:39
  131.0 2.2 %scatter_custom_fusion.1 = f32[2048,128]{1,0:T(8,128)S(1)} fusion(s32[384]{0:T(512)S(1)} %fusion.17, f32[]{:T(128)} %constant.11.clone.1, f32[384,128]{1,0:T(8,128)S(1)} %bitcast.21, f32[384]{0:T(512)S(1)} %reshape.122), kind=kCustom, calls=%fused_computation.13 | custom fusion | flops 98304 | bytes 1247236 | tf_op jit(solution)/shard_map/scatter-add | solution.py:43
  133.2 1.3 reshape.120
  134.5 0.0 all-reduce.2.cloned.1.call-update
  134.5 35.3 %all-reduce.2.cloned.1.call-done = f32[1024,256]{1,0:T(8,128)} async-done(((f32[1024,256]{1,0:T(8,128)}), f32[1024,256]{1,0:T(8,128)}) %all-reduce.2.cloned.1.call-update) | async-done | bytes 1048592 | tf_op jit(solution)/shard_map/psum | solution.py:45
  169.8 0.0 copy-done
  169.8 1.7 multiply_reduce_fusion
  171.5 2.7 %subtract_multiply_fusion = f32[1024,256]{1,0:T(8,128)} fusion(f32[1024,256]{1,0:T(8,128)} %all-reduce.2.cloned.1.call-done, f32[1024]{0:T(1024)S(1)} %multiply_reduce_fusion, f32[1024]{0:T(1024)S(1)} %fusion.5, f32[1024,256]{1,0:T(8,128)S(1)} %copy-done, f32[1024]{0:T(1024)S(1)} %reduce_max.9), kind=kLoop, calls=%fused_computation.8 | loop fusion | flops 1048576 | bytes 3158016 | tf_op jit(solution)/shard_map/mul | solution.py:46
  (3 shorter events, 0.0 us)
Async XLA Ops:
  7.2 81.6 %reduce-scatter.2.cloned.1.call-start = ((), (), s32[]{:S(2)}) async-start(), calls=%async_computation.1 | async-start | bytes 294912 | tf_op jit(solution)/shard_map/reduce_scatter | solution.py:34
  14.0 10.7 %copy-start.1 = (s32[1,8192]{1,0:T(1,128)S(1)}, s32[1,8192]{1,0:T(1,128)}, u32[]{:S(2)}) copy-start(s32[1,8192]{1,0:T(1,128)} %param.11) | copy-start | bytes 98308
  22.1 147.8 %copy-start = (f32[1024,256]{1,0:T(8,128)S(1)}, f32[1024,256]{1,0:T(8,128)}, u32[]{:S(2)}) copy-start(f32[1024,256]{1,0:T(8,128)} %param.6) | copy-start | bytes 3145732
  24.7 145.1 %all-reduce.2.cloned.1.call-start = ((), (), s32[]{:S(2)}) async-start(), calls=%async_computation.2 | async-start | bytes 2097152 | tf_op jit(solution)/shard_map/psum | solution.py:45
Sparse Core Ops, SparseCore 0:
  24.8 63.9 reduce-scatter.1
  134.7 35.0 all-reduce.1
where the time goes:
time: 181 us
  waiting for transfers between devices  99.3 us (55%)
  blocking collectives  30.5 us (17%)
  other arithmetic  16.8 us (9%)
  matrix products  15.8 us (9%)
  between operations  14.1 us (8%)
  local copies, waits for them, and re-layouts  4.42 us (2%)
    reduce_scatter x1, waiting for transfers between devices, shards(): lax.psum_scatter(partial_value, 'nets', scatter_dimension=0, tiled=True)  64 us
    psum x1, waiting for transfers between devices, shards(): summed_grad = lax.psum(local_grad.reshape(logits.shape), 'region')  35.3 us
    all_gather x1, blocking collectives, shards(): all_grads = lax.all_gather(edge_grad, 'nets', axis=0, tiled=True)  30.5 us
    dot_general x1, matrix products, shards(): jnp.einsum('tqe,te->tq', tile_block, slot_grads, preferred_element_type=j...  9.46 us
    dot_general x1, matrix products, shards(): jnp.einsum('tq,tqe->te', picked, tile_block, preferred_element_type=jnp.f...  6.35 us
  transfers between devices with their start and end apart: 2, of which 2 were waited for; matrix products, arithmetic and copies ran while one was open for 0% of the time, Pallas kernels for 0%

commit v1 on v0

--- a/solution.py
+++ b/solution.py
@@ -33,7 +33,22 @@
     )
     usage_edges = lax.psum_scatter(partial_value, "nets", scatter_dimension=0, tiled=True)
     edge_grad = jax.nn.sigmoid(usage_edges - capacity_f).astype(jnp.bfloat16)
-    all_grads = lax.all_gather(edge_grad, "nets", axis=0, tiled=True)
+    size, index, rows = (lax.axis_size("nets"), lax.axis_index("nets"), edge_grad.shape[0])
+    ahead = [(i, (i + 1) % size) for i in range(size)]
+    downward = [(i, (i - 1) % size) for i in range(size)]
+    out = jnp.zeros((*edge_grad.shape[:0], size * rows, *edge_grad.shape[0 + 1 :]), edge_grad.dtype)
+    out = lax.dynamic_update_slice_in_dim(out, edge_grad, index * rows, axis=0)
+    from_left = from_right = edge_grad
+    halfway = size // 2
+    for step in range(1, halfway + 1):
+        from_left = lax.ppermute(from_left, "nets", ahead)
+        out = lax.dynamic_update_slice_in_dim(out, from_left, (index - step) % size * rows, axis=0)
+        if step < size - halfway:
+            from_right = lax.ppermute(from_right, "nets", downward)
+            out = lax.dynamic_update_slice_in_dim(
+                out, from_right, (index + step) % size * rows, axis=0
+            )
+    all_grads = out
     slot_grads = all_grads[target]
     dp_tiles = (
         jnp.einsum("tqe,te->tq", tile_block, slot_grads, preferred_element_type=jnp.float32)

time: 181 us -> 174 us (0.961)
  blocking collectives: 30.5 us -> 0 us
  starting transfers between devices: 0.08 us -> 14.3 us
  waiting for transfers between devices: 99.3 us -> 109 us
    all_gather x1 -> x0, blocking collectives: 30.5 us -> none  [shards(): all_grads = lax.all_gather(edge_grad, 'nets', axis=0, tiled=True)]
    ppermute x0 -> x7, starting transfers between devices: none -> 14.2 us  [the longest x3 12.7 us: shards(): from_right = lax.ppermute(from_right, 'nets', downward)]
    ppermute x0 -> x7, waiting for transfers between devices: none -> 11.6 us  [the longest x4 11.6 us: shards(): from_left = lax.ppermute(from_left, 'nets', ahead)]
    psum x1, waiting for transfers between devices: 35.3 us -> 33.4 us  [shards(): summed_grad = lax.psum(local_grad.reshape(logits.shape), 'region')]
  transfers between devices with their start and end apart: 2 -> 9, of which waited for: 2 -> 6; matrix products, arithmetic and copies ran while one was open for 0% -> 0% of each run, Pallas kernels for 0% -> 0%
where the time goes in v1:
time: 174 us
  waiting for transfers between devices  109 us (63%)
  other arithmetic  16.1 us (9%)
  matrix products  15.8 us (9%)
  starting transfers between devices  14.3 us (8%)
  between operations  14.1 us (8%)
  local copies, waits for them, and re-layouts  4.5 us (3%)
    reduce_scatter x1, waiting for transfers between devices, shards(): lax.psum_scatter(partial_value, 'nets', scatter_dimension=0, tiled=True)  64 us
    psum x1, waiting for transfers between devices, shards(): summed_grad = lax.psum(local_grad.reshape(logits.shape), 'region')  33.4 us
    ppermute x3, starting transfers between devices, shards(): from_right = lax.ppermute(from_right, 'nets', downward)  12.7 us
    ppermute x4, waiting for transfers between devices, shards(): from_left = lax.ppermute(from_left, 'nets', ahead)  11.6 us
    dot_general x1, matrix products, shards(): jnp.einsum('tqe,te->tq', tile_block, slot_grads, preferred_element_type=j...  9.46 us
    dot_general x1, matrix products, shards(): jnp.einsum('tq,tqe->te', picked, tile_block, preferred_element_type=jnp.f...  6.35 us
  transfers between devices with their start and end apart: 9, of which 6 were waited for; matrix products, arithmetic and copies ran while one was open for 0% of the time, Pallas kernels for 0%

profile of v1, /device:TPU:0, one launch (start us, length us, event | category | flops | bytes accessed | tf_op | source)
XLA Modules:
  0.0 173.9 jit_solution(13941080090100039906)
XLA Ops:
  7.2 0.0 reduce-scatter.2.cloned.1.call-start
  7.2 1.4 reduce_max.9
  8.7 1.6 fusion.5
  10.2 0.7 fusion.16
  11.0 0.1 reshape.122
  11.0 0.7 fusion.17
  11.8 1.6 fusion.21
  13.4 0.0 copy-start.1
  13.4 0.2 reshape.119
  13.6 1.4 gather_fusion
  15.0 6.4 %fusion.2 = f32[384,1,128]{2,1,0:T(1,128)S(1)} fusion(bf16[1,1,384,128,128]{4,3,2,1,0:T(8,128)(2,1)} %param.7, bf16[384,128,1]{1,0,2:T(8,128)(2,1)S(1)} %bitcast.18), kind=kOutput, calls=%fused_computation.6 | convolution fusion | flops 12582912 | bytes 12877824 | tf_op jit(solution)/shard_map/tq,tqe->te/dot_general | solution.py:24
  21.4 0.0 copy-start
  21.4 2.6 %scatter_custom_fusion = f32[512,128]{1,0:T(8,128)} fusion(s32[384]{0:T(512)S(1)} %get-tuple-element.5, f32[384,128]{1,0:T(8,128)S(1)} %bitcast.19, f32[]{:T(128)} %constant.68.clone.1, f32[384]{0:T(512)S(1)} %reshape.122), kind=kCustom, calls=%fused_computation.18 | custom fusion | flops 98304 | bytes 460804 | tf_op jit(solution)/shard_map/scatter-add | solution.py:32
  24.0 0.0 reduce-scatter.2.cloned.1.call-update
  24.0 0.0 all-reduce.2.cloned.1.call-start
  24.1 0.0 copy-done.1
  24.1 64.0 %reduce-scatter.2.cloned.1.call-done = f32[64,128]{1,0:T(8,128)} async-done(((f32[512,128]{1,0:T(8,128)}), f32[64,128]{1,0:T(8,128)}) %reduce-scatter.2.cloned.1.call-update) | async-done | bytes 32784 | tf_op jit(solution)/shard_map/reduce_scatter | solution.py:34
  88.1 0.8 constant_dynamic-update-slice_fusion.7
  88.9 1.5 collective-permute-start
  90.4 3.3 %collective-permute-start.1 = (bf16[64,128]{1,0:T(8,128)(2,1)S(1)}, bf16[64,128]{1,0:T(8,128)(2,1)S(1)}, u32[]{:S(2)}, u32[]{:S(2)}) collective-permute-start(bf16[64,128]{1,0:T(8,128)(2,1)S(1)} %get-tuple-element.3), channel_id=1, source_target_pairs={{0,28},{4,0},{8,4},{12,8},{16,12},{20,16},{24,20},{28,24},{1,29},{... | collective-permute-start | bytes 49160 | tf_op jit(solution)/shard_map/ppermute | solution.py:47
  93.7 1.7 collective-permute-done
  95.4 0.0 collective-permute-start.2
  95.4 0.0 collective-permute-done.1
  95.4 4.7 %collective-permute-start.3 = (bf16[64,128]{1,0:T(8,128)(2,1)S(1)}, bf16[64,128]{1,0:T(8,128)(2,1)S(1)}, u32[]{:S(2)}, u32[]{:S(2)}) collective-permute-start(bf16[64,128]{1,0:T(8,128)(2,1)S(1)} %collective-permute-done.1), channel_id=1, source_target_pairs={{0,28},{4,0},{8,4},{12,8},{16,12},{20,16},{24,20},{28,24},{1,29},{... | collective-permute-start | bytes 49160 | tf_op jit(solution)/shard_map/ppermute | solution.py:47
  100.2 1.7 collective-permute-done.2
  101.9 0.0 collective-permute-start.4
  101.9 0.0 collective-permute-done.3
  101.9 4.7 %collective-permute-start.5 = (bf16[64,128]{1,0:T(8,128)(2,1)S(1)}, bf16[64,128]{1,0:T(8,128)(2,1)S(1)}, u32[]{:S(2)}, u32[]{:S(2)}) collective-permute-start(bf16[64,128]{1,0:T(8,128)(2,1)S(1)} %collective-permute-done.3), channel_id=1, source_target_pairs={{0,28},{4,0},{8,4},{12,8},{16,12},{20,16},{24,20},{28,24},{1,29},{... | collective-permute-start | bytes 49160 | tf_op jit(solution)/shard_map/ppermute | solution.py:47
  106.6 1.8 %collective-permute-done.4 = bf16[64,128]{1,0:T(8,128)(2,1)S(1)} collective-permute-done((bf16[64,128]{1,0:T(8,128)(2,1)S(1)}, bf16[64,128]{1,0:T(8,128)(2,1)S(1)}, u32[]{:S(2)}, u32[]{:S(2)}) %collective-permute-start.4) | collective-permute-done | bytes 16416 | tf_op jit(solution)/shard_map/ppermute | solution.py:44
  108.4 0.0 collective-permute-start.6
  108.4 0.0 collective-permute-done.5
  108.5 6.4 %collective-permute-done.6 = bf16[64,128]{1,0:T(8,128)(2,1)S(1)} collective-permute-done((bf16[64,128]{1,0:T(8,128)(2,1)S(1)}, bf16[64,128]{1,0:T(8,128)(2,1)S(1)}, u32[]{:S(2)}, u32[]{:S(2)}) %collective-permute-start.6) | collective-permute-done | bytes 16416 | tf_op jit(solution)/shard_map/ppermute | solution.py:44
  114.9 1.4 gather_fusion.1
  116.3 9.5 %fusion = f32[384,1,128]{2,1,0:T(1,128)S(1)} fusion(bf16[1,1,384,128,128]{4,3,2,1,0:T(8,128)(2,1)} %param.7, bf16[384,128,1]{1,0,2:T(8,128)(2,1)S(1)} %bitcast.20), kind=kOutput, calls=%fused_computation.4 | convolution fusion | flops 12582912 | bytes 12877824 | tf_op jit(solution)/shard_map/tqe,te->tq/dot_general | solution.py:54
  125.8 2.2 %scatter_custom_fusion.1 = f32[2048,128]{1,0:T(8,128)S(1)} fusion(s32[384]{0:T(512)S(1)} %get-tuple-element.4, f32[]{:T(128)} %constant.68.clone.1, f32[384,128]{1,0:T(8,128)S(1)} %bitcast.21, f32[384]{0:T(512)S(1)} %reshape.122), kind=kCustom, calls=%fused_computation.13 | custom fusion | flops 98304 | bytes 1247236 | tf_op jit(solution)/shard_map/scatter-add | solution.py:58
  128.0 1.3 reshape.120
  129.3 0.0 all-reduce.2.cloned.1.call-update
  129.3 33.4 %all-reduce.2.cloned.1.call-done = f32[1024,256]{1,0:T(8,128)} async-done(((f32[1024,256]{1,0:T(8,128)}), f32[1024,256]{1,0:T(8,128)}) %all-reduce.2.cloned.1.call-update) | async-done | bytes 1048592 | tf_op jit(solution)/shard_map/psum | solution.py:60
  162.7 0.0 copy-done
  162.7 1.7 multiply_reduce_fusion
  164.4 2.7 %subtract_multiply_fusion = f32[1024,256]{1,0:T(8,128)} fusion(f32[1024,256]{1,0:T(8,128)} %all-reduce.2.cloned.1.call-done, f32[1024]{0:T(1024)S(1)} %multiply_reduce_fusion, f32[1024]{0:T(1024)S(1)} %fusion.5, f32[1024,256]{1,0:T(8,128)S(1)} %copy-done, f32[1024]{0:T(1024)S(1)} %reduce_max.9), kind=kLoop, calls=%fused_computation.8 | loop fusion | flops 1048576 | bytes 3158016 | tf_op jit(solution)/shard_map/mul | solution.py:61
  (11 shorter events, 0.1 us)
Async XLA Ops:
  7.2 81.0 %reduce-scatter.2.cloned.1.call-start = ((), (), s32[]{:S(2)}) async-start(), calls=%async_computation.1 | async-start | bytes 294912 | tf_op jit(solution)/shard_map/reduce_scatter | solution.py:34
  13.4 10.7 %copy-start.1 = (s32[1,8192]{1,0:T(1,128)S(1)}, s32[1,8192]{1,0:T(1,128)}, u32[]{:S(2)}) copy-start(s32[1,8192]{1,0:T(1,128)} %param.11) | copy-start | bytes 98308
  21.4 141.3 %copy-start = (f32[1024,256]{1,0:T(8,128)S(1)}, f32[1024,256]{1,0:T(8,128)}, u32[]{:S(2)}) copy-start(f32[1024,256]{1,0:T(8,128)} %param.6) | copy-start | bytes 3145732
  24.0 138.7 %all-reduce.2.cloned.1.call-start = ((), (), s32[]{:S(2)}) async-start(), calls=%async_computation.2 | async-start | bytes 2097152 | tf_op jit(solution)/shard_map/psum | solution.py:60
  88.9 6.5 %collective-permute-start = (bf16[64,128]{1,0:T(8,128)(2,1)S(1)}, bf16[64,128]{1,0:T(8,128)(2,1)S(1)}, u32[]{:S(2)}, u32[]{:S(2)}) collective-permute-start(bf16[64,128]{1,0:T(8,128)(2,1)S(1)} %get-tuple-element.3), channel_id=1, source_target_pairs={{0,4},{4,8},{8,12},{12,16},{16,20},{20,24},{24,28},{28,0},{1,5},{5... | collective-permute-start | bytes 49160 | tf_op jit(solution)/shard_map/ppermute | solution.py:44
  90.4 5.0 %collective-permute-start.1 = (bf16[64,128]{1,0:T(8,128)(2,1)S(1)}, bf16[64,128]{1,0:T(8,128)(2,1)S(1)}, u32[]{:S(2)}, u32[]{:S(2)}) collective-permute-start(bf16[64,128]{1,0:T(8,128)(2,1)S(1)} %get-tuple-element.3), channel_id=1, source_target_pairs={{0,28},{4,0},{8,4},{12,8},{16,12},{20,16},{24,20},{28,24},{1,29},{... | collective-permute-start | bytes 49160 | tf_op jit(solution)/shard_map/ppermute | solution.py:47
  95.4 6.4 %collective-permute-start.2 = (bf16[64,128]{1,0:T(8,128)(2,1)S(1)}, bf16[64,128]{1,0:T(8,128)(2,1)S(1)}, u32[]{:S(2)}, u32[]{:S(2)}) collective-permute-start(bf16[64,128]{1,0:T(8,128)(2,1)S(1)} %collective-permute-done), channel_id=1, source_target_pairs={{0,4},{4,8},{8,12},{12,16},{16,20},{20,24},{24,28},{28,0},{1,5},{5... | collective-permute-start | bytes 49160 | tf_op jit(solution)/shard_map/ppermute | solution.py:44
  95.4 6.4 %collective-permute-start.3 = (bf16[64,128]{1,0:T(8,128)(2,1)S(1)}, bf16[64,128]{1,0:T(8,128)(2,1)S(1)}, u32[]{:S(2)}, u32[]{:S(2)}) collective-permute-start(bf16[64,128]{1,0:T(8,128)(2,1)S(1)} %collective-permute-done.1), channel_id=1, source_target_pairs={{0,28},{4,0},{8,4},{12,8},{16,12},{20,16},{24,20},{28,24},{1,29},{... | collective-permute-start | bytes 49160 | tf_op jit(solution)/shard_map/ppermute | solution.py:47
  101.9 6.6 %collective-permute-start.4 = (bf16[64,128]{1,0:T(8,128)(2,1)S(1)}, bf16[64,128]{1,0:T(8,128)(2,1)S(1)}, u32[]{:S(2)}, u32[]{:S(2)}) collective-permute-start(bf16[64,128]{1,0:T(8,128)(2,1)S(1)} %collective-permute-done.2), channel_id=1, source_target_pairs={{0,4},{4,8},{8,12},{12,16},{16,20},{20,24},{24,28},{28,0},{1,5},{5... | collective-permute-start | bytes 49160 | tf_op jit(solution)/shard_map/ppermute | solution.py:44
  101.9 6.6 %collective-permute-start.5 = (bf16[64,128]{1,0:T(8,128)(2,1)S(1)}, bf16[64,128]{1,0:T(8,128)(2,1)S(1)}, u32[]{:S(2)}, u32[]{:S(2)}) collective-permute-start(bf16[64,128]{1,0:T(8,128)(2,1)S(1)} %collective-permute-done.3), channel_id=1, source_target_pairs={{0,28},{4,0},{8,4},{12,8},{16,12},{20,16},{24,20},{28,24},{1,29},{... | collective-permute-start | bytes 49160 | tf_op jit(solution)/shard_map/ppermute | solution.py:47
  108.4 6.4 %collective-permute-start.6 = (bf16[64,128]{1,0:T(8,128)(2,1)S(1)}, bf16[64,128]{1,0:T(8,128)(2,1)S(1)}, u32[]{:S(2)}, u32[]{:S(2)}) collective-permute-start(bf16[64,128]{1,0:T(8,128)(2,1)S(1)} %collective-permute-done.4), channel_id=1, source_target_pairs={{0,4},{4,8},{8,12},{12,16},{16,20},{20,24},{24,28},{28,0},{1,5},{5... | collective-permute-start | bytes 49160 | tf_op jit(solution)/shard_map/ppermute | solution.py:44
Sparse Core Ops, SparseCore 0:
  24.1 63.9 reduce-scatter.1
  129.4 33.2 all-reduce.1
